TPU v7x, 512 devices: a whole 4x8x8 slice. The times are simulated.
512 devices in a mesh: owner: 16 (over x, y_hi), beam: 32 (over y_lo, z, core).
Axes of the slice: x: 4, y: 8 (y_hi: 4, y_lo: 2; y = y_hi * 2 + y_lo), z: 8, core: 2. Of those that a mesh axis runs over, the one named last changes fastest.
Arguments:
- hidden: bfloat16 [4096, 8192], P('owner'), may hold values from -6 to 6
- norm_gain: bfloat16 [8192], replicated, may hold values from 0.099609375 to 1.8984375
- w_qkv: bfloat16 [8192, 10240], P('owner', 'beam'), may hold values from -0.0625 to 0.0625
- w_out: bfloat16 [8192, 8192], P('beam', 'owner'), may hold values from -0.125 to 0.125
- kv_cache: bfloat16 [16384, 2, 8, 1024], P(('owner', 'beam')), may hold values from -384 to 384
- lengths: int32 [4096], P('owner'), may hold values from 1 to 32, 98304 in all
- kept_parent_device: int32 [16384, 1], P('owner'), may hold values from 0 to 31; in each aligned block of 32 rows (0 to 31, 32 to 63, ...) at most 2 rows name the same one
- keep_block: int32 [16384], P('owner'), may hold values from 0 to 31
Outputs:
- mixed: bfloat16 [4096, 8192], P('owner', 'beam')
Inputs may be any that keep to these rules, and one draw needn't show every extreme that they name: `kept_parent_device`: in each aligned block of 32 entries (the new blocks of one device) no value appears more than 2 times, and some value appears exactly 2 times in some block. `lengths`: each entry is at least 1; the largest is exactly 32.
All inputs are finite; a program needn't handle non-finite values. No bound on the sum of `lengths` on one device may be relied on, other than what follows from the above.
Results may differ from a plain program's by a relative error of at most 0.024.
Values may be sent and summed in bfloat16 or wider, within the bound.
No kernel may reach another device: no remote copies, remote signals or barrier semaphores. Data moves between devices by JAX's collectives and lax.ppermute only.
A program may use at most 64 MiB of HBM per device.

v0:
```python
import jax
import jax.numpy as jnp
from jax import lax
from jax.sharding import PartitionSpec as P

QH = 64
KVH = 8
HD = 128
CACHE = 32
PAGE = 8
QKV = 10240


def rotary_embed(values, positions):
    half = values.shape[-1] // 2
    freqs = 500000.0 ** (-(jnp.arange(half, dtype=jnp.float32) * 2.0) / values.shape[-1])
    angles = positions.astype(jnp.float32)[:, None] * freqs[None, :]
    cosine = jnp.cos(angles)[:, None, :]
    sine = jnp.sin(angles)[:, None, :]
    first = values[..., :half]
    second = values[..., half:]
    return jnp.concatenate(
        [first * cosine - second * sine, second * cosine + first * sine], axis=-1
    )


def regroup(blocks):
    return lax.all_to_all(blocks, "beam", split_axis=1, concat_axis=1, tiled=True)


def attend(queries, fresh_key, value_new, keys, values, positions):
    beams = queries.shape[0]
    grouped_heads = queries.reshape(beams, KVH, QH // KVH, HD)
    scale_factor = HD ** (-0.5)
    scores = (
        jnp.einsum("bkgd,btkd->bkgt", grouped_heads, keys, preferred_element_type=jnp.float32)
        * scale_factor
    )
    local_beam_score = (
        jnp.einsum("rhap,rhp->rha", grouped_heads, fresh_key, preferred_element_type=jnp.float32)
        * scale_factor
    )
    valid = (jnp.arange(keys.shape[1], dtype=jnp.int32)[None, :] < positions[:, None])[
        :, None, None, :
    ]
    scores = jnp.where(valid, scores, -1e30)
    highest = jnp.maximum(jnp.max(scores, axis=-1), local_beam_score)
    weights = jnp.where(valid, jnp.exp(scores - highest[..., None]), 0.0)
    own_weight = jnp.exp(local_beam_score - highest)
    totals = jnp.sum(weights, axis=-1) + own_weight
    probs = (weights / totals[..., None]).astype(jnp.bfloat16)
    own_prob = (own_weight / totals).astype(jnp.bfloat16)
    output = jnp.einsum("bkgt,btkd->bkgd", probs, values, preferred_element_type=jnp.float32)
    output = (
        output
        + own_prob.astype(jnp.float32)[..., None] * value_new.astype(jnp.float32)[:, :, None, :]
    )
    return output.reshape(beams, QH * HD).astype(jnp.bfloat16)


def shards(hidden, norm_gain, w_qkv, w_out, kv_cache, lengths, kept_parent_device, keep_block):
    columns = lax.axis_size("beam")
    my_column = lax.axis_index("beam")
    grouped_row_block = hidden.shape[0]
    own_beams = grouped_row_block // columns
    floats = hidden.astype(jnp.float32)
    scale_rms = lax.rsqrt(jnp.mean(floats * floats, axis=-1, keepdims=True) + 1e-05)
    normed = (floats * scale_rms * norm_gain.astype(jnp.float32)).astype(jnp.bfloat16)
    normed_split = normed.reshape(columns, own_beams, normed.shape[1])
    projected = jnp.einsum(
        "jbd,dc->bjc",
        normed_split,
        lax.all_gather(w_qkv, "owner", axis=0, tiled=True),
        preferred_element_type=jnp.float32,
    )
    own_qkv = regroup(projected.astype(jnp.bfloat16)).reshape(own_beams, QKV)
    blk_dev = kv_cache.shape[0]
    most_slots = max(2, 2 * blk_dev // columns)
    sources = kept_parent_device.reshape(columns, blk_dev)
    picked = keep_block.reshape(columns, blk_dev)
    is_mine = (sources == my_column).astype(jnp.int32)
    ranks = jnp.cumsum(is_mine, axis=1) - 1
    slot_ids = jnp.arange(most_slots, dtype=jnp.int32)
    chosen = is_mine[:, :, None] * (ranks[:, :, None] == slot_ids[None, None, :]).astype(jnp.int32)
    send_table = jnp.sum(chosen * picked[:, :, None], axis=1)
    outgoing = kv_cache[send_table.reshape(-1)].reshape((columns, most_slots) + kv_cache.shape[1:])
    incoming_blocks = lax.all_to_all(outgoing, "beam", split_axis=0, concat_axis=0, tiled=True)
    own_sources = lax.dynamic_index_in_dim(sources, my_column, 0, keepdims=False)
    one_hot = (own_sources[:, None] == jnp.arange(columns, dtype=jnp.int32)[None, :]).astype(
        jnp.int32
    )
    earlier = jnp.cumsum(one_hot, axis=0) - one_hot
    arrival = jnp.sum(earlier * one_hot, axis=1)
    flat_blocks = incoming_blocks.reshape((columns * most_slots,) + kv_cache.shape[1:])
    moved = flat_blocks[own_sources * most_slots + arrival]
    moved = moved.reshape(own_beams, CACHE // PAGE, 2, PAGE, KVH, HD)
    keys = moved[:, :, 0].reshape(own_beams, CACHE, KVH, HD)
    values = moved[:, :, 1].reshape(own_beams, CACHE, KVH, HD)
    positions = lax.dynamic_slice_in_dim(lengths, my_column * own_beams, own_beams)
    query_cols = own_qkv[:, : QH * HD].reshape(own_beams, QH, HD).astype(jnp.float32)
    key_cols = own_qkv[:, QH * HD : (QH + KVH) * HD].reshape(own_beams, KVH, HD).astype(jnp.float32)
    value_new = own_qkv[:, (QH + KVH) * HD :].reshape(own_beams, KVH, HD)
    queries = rotary_embed(query_cols, positions).astype(jnp.bfloat16)
    fresh_key = rotary_embed(key_cols, positions).astype(jnp.bfloat16)
    attn = attend(queries, fresh_key, value_new, keys, values, positions)
    head_rows = regroup(attn.reshape(own_beams, columns, attn.shape[1] // columns))
    w_piece = lax.all_gather(w_out, "owner", axis=1, tiled=True)
    terms = jnp.einsum(
        "bjh,hc->jbc", head_rows, w_piece, preferred_element_type=jnp.float32
    ).reshape(grouped_row_block, w_piece.shape[1])
    return lax.psum_scatter(terms.astype(jnp.bfloat16), "beam", scatter_dimension=1, tiled=True)


def solution(mesh):
    return jax.shard_map(
        shards,
        mesh=mesh,
        in_specs=(
            P("owner", None),
            P(),
            P("owner", "beam"),
            P("beam", "owner"),
            P(("owner", "beam"), None, None, None),
            P("owner"),
            P("owner", None),
            P("owner"),
        ),
        out_specs=P("owner", "beam"),
        check_vma=False,
    )
```

profile of v0, /device:TPU:2, one launch (start us, length us, event | category | flops | bytes accessed | tf_op | source)
XLA Modules:
  0.0 348.0 jit_solution(10896632046652622338)
XLA Ops:
  6.5 0.7 all-gather.3.cloned.1.call-update
  7.3 0.7 all-gather.5.cloned.1.call-update
  8.0 0.5 broadcast.155
  8.5 1.3 reduce.3
  10.0 0.2 reduce_window_sum.22
  10.1 0.8 mul.193
  10.9 0.1 multiply_reduce_fusion
  11.1 0.1 reshape.207
  11.3 2.0 gather_fusion
  13.3 11.7 %all-to-all-start.1 = ((bf16[32,2,2,8,1024]{4,3,2,1,0:T(8,128)(2,1)}), bf16[32,2,2,8,1024]{4,3,2,1,0:T(8,128)(2,1)S(1)}, u32[]{:S(2)}, u32[]{:S(2)}) async-start(bf16[32,2,2,8,1024]{4,3,2,1,0:T(8,128)(2,1)} %bitcast.8), calls=%async_computation.1 | async-start | bytes 4194304 | tf_op jit(solution)/shard_map/all_to_all | solution.py:87
  25.3 0.2 select_reduce_fusion
  25.6 3.1 fusion.1
  28.7 0.1 multiply_cosine_fusion
  28.8 88.1 %all-gather.3.cloned.1.call-done = bf16[8192,320]{0,1:T(8,128)(2,1)} async-done(((bf16[512,320]{0,1:T(8,128)(2,1)}), bf16[8192,320]{0,1:T(8,128)(2,1)}) %all-gather.3.cloned.1.call-update) | async-done | bytes 5242896 | tf_op jit(solution)/shard_map/all_gather | solution.py:73
  116.9 6.8 %fusion.18 = bf16[8,32,320]{2,0,1:T(8,128)(2,1)} fusion(bf16[8192,320]{0,1:T(8,128)(2,1)} %all-gather.3.cloned.1.call-done, bf16[256,8192]{1,0:T(8,128)(2,1)} %param.8, f32[8192]{0:T(1024)S(1)} %convert_element_type.85, f32[256]{0:T(256)S(1)} %add_rsqrt_fusion), kind=kOutput, calls=%fused_computation.21 | convolution fusion | flops 1350647808 | bytes 9634816 | tf_op jit(solution)/shard_map/jbd,dc->bjc/dot_general | solution.py:70
  123.7 10.2 %all-to-all-start = ((bf16[8,32,320]{2,0,1:T(8,128)(2,1)}), bf16[8,32,320]{2,0,1:T(8,128)(2,1)S(1)}, u32[]{:S(2)}, u32[]{:S(2)}) async-start(bf16[8,32,320]{2,0,1:T(8,128)(2,1)} %fusion.18), calls=%async_computation | async-start | bytes 393216 | tf_op jit(solution)/shard_map/all_to_all | solution.py:28
  133.9 1.6 gather_fusion.1
  135.5 1.5 copy.39
  137.2 6.6 %all-to-all-done = bf16[8,32,320]{2,0,1:T(8,128)(2,1)S(1)} async-done(((bf16[8,32,320]{2,0,1:T(8,128)(2,1)}), bf16[8,32,320]{2,0,1:T(8,128)(2,1)S(1)}, u32[]{:S(2)}, u32[]{:S(2)}) %all-to-all-start) | async-done | bytes 163872 | tf_op jit(solution)/shard_map/all_to_all | solution.py:28
  143.8 0.2 reshape.205
  144.3 0.1 fusion.51
  144.4 0.1 fusion.28
  144.5 0.3 fusion.36
  144.8 0.5 fusion.52
  145.3 0.3 fusion.27
  145.6 0.3 fusion.17
  146.0 0.7 copy.32
  146.8 4.3 %all-to-all-start.2 = ((bf16[8,32,256]{2,0,1:T(8,128)(2,1)}), bf16[8,32,256]{2,0,1:T(8,128)(2,1)S(1)}, u32[]{:S(2)}, u32[]{:S(2)}) async-start(bf16[8,32,256]{2,0,1:T(8,128)(2,1)} %copy.32), calls=%async_computation.2 | async-start | bytes 262144 | tf_op jit(solution)/shard_map/all_to_all | solution.py:28
  151.1 58.5 %all-gather.5.cloned.1.call-done = bf16[256,8192]{1,0:T(8,128)(2,1)} async-done(((bf16[256,512]{1,0:T(8,128)(2,1)}), bf16[256,8192]{1,0:T(8,128)(2,1)}) %all-gather.5.cloned.1.call-update) | async-done | bytes 4194320 | tf_op jit(solution)/shard_map/all_gather | solution.py:107
  209.6 3.4 fusion
  213.0 4.2 %copy.67 = bf16[32,8,8192]{2,1,0:T(8,128)(2,1)} copy(bf16[32,8,8192]{2,0,1:T(8,128)(2,1)S(1)} %fusion) | data formatting | bytes 8388608 | tf_op jit(solution)/shard_map/convert_element_type | solution.py:111
  217.3 124.2 %reduce-scatter.2.cloned.1.call-done = bf16[256,256]{1,0:T(8,128)(2,1)} async-done(((bf16[256,8192]{1,0:T(8,128)(2,1)}), bf16[256,256]{1,0:T(8,128)(2,1)}) %reduce-scatter.2.cloned.1.call-update) | async-done | bytes 131088 | tf_op jit(solution)/shard_map/reduce_scatter | solution.py:111
  (38 shorter events, 1.0 us)
Async XLA Ops:
  6.5 4.7 %copy-start = (bf16[32,2,8,1024]{3,2,1,0:T(8,128)(2,1)S(1)}, bf16[32,2,8,1024]{3,2,1,0:T(8,128)(2,1)}, u32[]{:S(2)}) copy-start(bf16[32,2,8,1024]{3,2,1,0:T(8,128)(2,1)} %param.12) | copy-start | bytes 3145732
  6.5 110.3 %all-gather.3.cloned.1.call-start = ((), (), s32[]{:S(2)}) async-start(), calls=%async_computation.4 | async-start | bytes 5570560 | tf_op jit(solution)/shard_map/all_gather | solution.py:73
  7.3 202.3 %all-gather.5.cloned.1.call-start = ((), (), s32[]{:S(2)}) async-start(), calls=%async_computation.5 | async-start | bytes 4456448 | tf_op jit(solution)/shard_map/all_gather | solution.py:107
  11.3 13.8 %copy-start.1 = (bf16[8192]{0:T(1024)(128)(2,1)S(1)}, bf16[8192]{0:T(1024)(128)(2,1)}, u32[]{:S(2)}) copy-start(bf16[8192]{0:T(1024)(128)(2,1)} %param.9) | copy-start | bytes 49156
  11.3 13.9 %copy-start.2 = (s32[256]{0:T(256)S(1)}, s32[256]{0:T(256)}, u32[]{:S(2)}) copy-start(s32[256]{0:T(256)} %param.13) | copy-start | bytes 3076
  13.3 110.4 %all-to-all-start.1 = ((bf16[32,2,2,8,1024]{4,3,2,1,0:T(8,128)(2,1)}), bf16[32,2,2,8,1024]{4,3,2,1,0:T(8,128)(2,1)S(1)}, u32[]{:S(2)}, u32[]{:S(2)}) async-start(bf16[32,2,2,8,1024]{4,3,2,1,0:T(8,128)(2,1)} %bitcast.8), calls=%async_computation.1 | async-start | bytes 4194304 | tf_op jit(solution)/shard_map/all_to_all | solution.py:87
  123.7 20.1 %all-to-all-start = ((bf16[8,32,320]{2,0,1:T(8,128)(2,1)}), bf16[8,32,320]{2,0,1:T(8,128)(2,1)S(1)}, u32[]{:S(2)}, u32[]{:S(2)}) async-start(bf16[8,32,320]{2,0,1:T(8,128)(2,1)} %fusion.18), calls=%async_computation | async-start | bytes 393216 | tf_op jit(solution)/shard_map/all_to_all | solution.py:28
  146.8 62.8 %all-to-all-start.2 = ((bf16[8,32,256]{2,0,1:T(8,128)(2,1)}), bf16[8,32,256]{2,0,1:T(8,128)(2,1)S(1)}, u32[]{:S(2)}, u32[]{:S(2)}) async-start(bf16[8,32,256]{2,0,1:T(8,128)(2,1)} %copy.32), calls=%async_computation.2 | async-start | bytes 262144 | tf_op jit(solution)/shard_map/all_to_all | solution.py:28
  151.0 190.4 %reduce-scatter.2.cloned.1.call-start = ((), (), s32[]{:S(2)}) async-start(), calls=%async_computation.6 | async-start | bytes 4325376 | tf_op jit(solution)/shard_map/reduce_scatter | solution.py:111
Sparse Core Ops, SparseCore 0:
  10.3 106.4 all-gather.2
  119.9 89.6 all-gather.4
  217.4 123.9 reduce-scatter.1
where the time goes:
time: 348 us
  waiting for transfers between devices  279 us (80%)
  starting transfers between devices  26.3 us (8%)
  between operations  13.3 us (4%)
  local copies, waits for them, and re-layouts  12.2 us (4%)
  matrix products  11.4 us (3%)
  other arithmetic  5.99 us (2%)
    reduce_scatter x1, waiting for transfers between devices, shards(): lax.psum_scatter(terms.astype(jnp.bfloat16), 'beam', scatter_dimension=1,...  124 us
    all_gather x1, waiting for transfers between devices, shards(): lax.all_gather(w_qkv, 'owner', axis=0, tiled=True)  88.1 us
    all_gather x1, waiting for transfers between devices, shards(): w_piece = lax.all_gather(w_out, 'owner', axis=1, tiled=True)  58.5 us
    all_to_all x2, starting transfers between devices, regroup(): lax.all_to_all(blocks, 'beam', split_axis=1, concat_axis=1, tiled=True)  14.5 us
    all_to_all x1, starting transfers between devices, shards(): lax.all_to_all(outgoing, 'beam', split_axis=0, concat_axis=0, tiled=True)  11.7 us
  transfers between devices with their start and end apart: 6, of which 4 were waited for; matrix products, arithmetic and copies ran while one was open for 6% of the time, Pallas kernels for 0%

commit v1 on v0

--- a/solution.py
+++ b/solution.py
@@ -9,6 +9,11 @@
 CACHE = 32
 PAGE = 8
 QKV = 10240
+
+
+def gather_over(block, axis, dim):
+    repeated = jnp.stack([block] * lax.axis_size(axis))
+    return jnp.concatenate(lax.all_to_all(repeated, axis, 0, 0), axis=dim)
 
 
 def rotary_embed(values, positions):
@@ -70,7 +75,7 @@
     projected = jnp.einsum(
         "jbd,dc->bjc",
         normed_split,
-        lax.all_gather(w_qkv, "owner", axis=0, tiled=True),
+        gather_over(w_qkv, "owner", 0),
         preferred_element_type=jnp.float32,
     )
     own_qkv = regroup(projected.astype(jnp.bfloat16)).reshape(own_beams, QKV)

time: 348 us -> 417 us (1.20)
  waiting for transfers between devices: 279 us -> 320 us
  local copies, waits for them, and re-layouts: 12.2 us -> 32 us
  starting transfers between devices: 26.3 us -> 33.8 us
    all_to_all x0 -> x1, waiting for transfers between devices: none -> 162 us  [gather_over(): return jnp.concatenate(lax.all_to_all(repeated, axis, 0, 0), axis=dim)]
    all_gather x1 -> x0, waiting for transfers between devices: 88.1 us -> none  [shards(): lax.all_gather(w_qkv, 'owner', axis=0, tiled=True)]
    all_gather x1, waiting for transfers between devices: 58.5 us -> 0.02 us  [shards(): w_piece = lax.all_gather(w_out, 'owner', axis=1, tiled=True)]
    all_to_all x1, waiting for transfers between devices: 0.01 us -> 23 us  [shards(): lax.all_to_all(outgoing, 'beam', split_axis=0, concat_axis=0, tiled=True)]
    all_to_all x0 -> x1, starting transfers between devices: none -> 10.4 us  [gather_over(): return jnp.concatenate(lax.all_to_all(repeated, axis, 0, 0), axis=dim)]
    all_to_all x2, waiting for transfers between devices: 6.61 us -> 15.6 us  [regroup(): lax.all_to_all(blocks, 'beam', split_axis=1, concat_axis=1, tiled=True)]
    reshape x0 -> x1, local copies, waits for them, and re-layouts: none -> 8.91 us  [gather_over(): return jnp.concatenate(lax.all_to_all(repeated, axis, 0, 0), axis=dim)]
    all_to_all x0 -> x1, local copies, waits for them, and re-layouts: none -> 7.77 us  [gather_over(): return jnp.concatenate(lax.all_to_all(repeated, axis, 0, 0), axis=dim)]
  transfers between devices with their start and end apart: 6 -> 6, of which waited for: 4 -> 5; matrix products, arithmetic and copies ran while one was open for 6% -> 9% of each run, Pallas kernels for 0% -> 0%
where the time goes in v1:
time: 417 us; the launch traced here: 416 us
  waiting for transfers between devices  320 us (77%)
  starting transfers between devices  33.8 us (8%)
  local copies, waits for them, and re-layouts  32 us (8%)
  between operations  13.7 us (3%)
  matrix products  11.4 us (3%)
  other arithmetic  5.3 us (1%)
    all_to_all x1, waiting for transfers between devices, gather_over(): return jnp.concatenate(lax.all_to_all(repeated, axis, 0, 0), axis=dim)  162 us
    reduce_scatter x1, waiting for transfers between devices, shards(): lax.psum_scatter(terms.astype(jnp.bfloat16), 'beam', scatter_dimension=1,...  118 us
    all_to_all x1, waiting for transfers between devices, shards(): lax.all_to_all(outgoing, 'beam', split_axis=0, concat_axis=0, tiled=True)  23 us
    all_to_all x2, waiting for transfers between devices, regroup(): lax.all_to_all(blocks, 'beam', split_axis=1, concat_axis=1, tiled=True)  15.6 us
    all_to_all x2, starting transfers between devices, regroup(): lax.all_to_all(blocks, 'beam', split_axis=1, concat_axis=1, tiled=True)  13 us
    all_to_all x1, starting transfers between devices, gather_over(): return jnp.concatenate(lax.all_to_all(repeated, axis, 0, 0), axis=dim)  10.4 us
    all_to_all x1, starting transfers between devices, shards(): lax.all_to_all(outgoing, 'beam', split_axis=0, concat_axis=0, tiled=True)  10.1 us
    reshape x1, local copies, waits for them, and re-layouts, gather_over(): return jnp.concatenate(lax.all_to_all(repeated, axis, 0, 0), axis=dim)  8.91 us
  transfers between devices with their start and end apart: 6, of which 5 were waited for; matrix products, arithmetic and copies ran while one was open for 9% of the time, Pallas kernels for 0%

profile of v1, /device:TPU:2, one launch (start us, length us, event | category | flops | bytes accessed | tf_op | source)
XLA Modules:
  0.0 415.9 jit_solution(8899453377193502243)
XLA Ops:
  6.5 3.9 stack.2
  10.4 10.4 %all-to-all-start = ((bf16[16,512,320]{1,2,0:T(8,128)(2,1)}), bf16[16,512,320]{1,2,0:T(8,128)(2,1)}, u32[]{:S(2)}, u32[]{:S(2)}) async-start(bf16[16,512,320]{1,2,0:T(8,128)(2,1)} %stack.2), calls=%async_computation | async-start | bytes 10485760 | tf_op jit(solution)/shard_map/all_to_all | solution.py:16
  20.9 0.7 all-gather.2.cloned.1.call-update
  21.6 0.5 broadcast.157
  22.1 0.7 reduce.3
  22.8 0.2 reduce_window_sum.22
  23.5 2.0 gather_fusion
  25.5 162.0 %all-to-all-done = bf16[16,512,320]{1,2,0:T(8,128)(2,1)} async-done(((bf16[16,512,320]{1,2,0:T(8,128)(2,1)}), bf16[16,512,320]{1,2,0:T(8,128)(2,1)}, u32[]{:S(2)}, u32[]{:S(2)}) %all-to-all-start) | async-done | bytes 5242912 | tf_op jit(solution)/shard_map/all_to_all | solution.py:16
  187.5 10.1 %all-to-all-start.2 = ((bf16[32,2,2,8,1024]{4,3,2,1,0:T(8,128)(2,1)}), bf16[32,2,2,8,1024]{4,3,2,1,0:T(8,128)(2,1)S(1)}, u32[]{:S(2)}, u32[]{:S(2)}) async-start(bf16[32,2,2,8,1024]{4,3,2,1,0:T(8,128)(2,1)} %bitcast.7), calls=%async_computation.2 | async-start | bytes 4194304 | tf_op jit(solution)/shard_map/all_to_all | solution.py:92
  197.9 0.2 select_reduce_fusion
  198.1 3.1 fusion.1
  201.4 7.8 %copy.26 = bf16[16,512,320]{1,0,2:T(8,128)(2,1)} copy(bf16[16,512,320]{1,2,0:T(8,128)(2,1)} %all-to-all-done) | data formatting | bytes 10485760 | tf_op jit(solution)/shard_map/all_to_all | solution.py:16
  209.1 8.9 %reshape.236 = bf16[8192,320,1]{0,1,2:T(8,128)(2,1)} reshape(bf16[16,512,320]{1,0,2:T(8,128)(2,1)} %copy.26) | data formatting | bytes 10485760 | tf_op jit(solution)/shard_map/reshape | solution.py:16
  218.1 6.8 %fusion.15 = bf16[8,32,320]{2,0,1:T(8,128)(2,1)} fusion(bf16[8192,320,1]{0,1,2:T(8,128)(2,1)} %reshape.236, bf16[256,8192]{1,0:T(8,128)(2,1)} %param.8, f32[8192]{0:T(1024)S(1)} %convert_element_type.85, f32[256]{0:T(256)S(1)} %add_rsqrt_fusion), kind=kOutput, calls=%fused_computation.20 | convolution fusion | flops 1350647808 | bytes 9634816 | tf_op jit(solution)/shard_map/jbd,dc->bjc/dot_general | solution.py:75
  224.9 23.0 %all-to-all-done.2 = bf16[32,2,2,8,1024]{4,3,2,1,0:T(8,128)(2,1)S(1)} async-done(((bf16[32,2,2,8,1024]{4,3,2,1,0:T(8,128)(2,1)}), bf16[32,2,2,8,1024]{4,3,2,1,0:T(8,128)(2,1)S(1)}, u32[]{:S(2)}, u32[]{:S(2)}) %all-to-all-start.2) | async-done | bytes 2097184 | tf_op jit(solution)/shard_map/all_to_all | solution.py:92
  247.9 8.8 %all-to-all-start.1 = ((bf16[8,32,320]{2,0,1:T(8,128)(2,1)}), bf16[8,32,320]{2,0,1:T(8,128)(2,1)S(1)}, u32[]{:S(2)}, u32[]{:S(2)}) async-start(bf16[8,32,320]{2,0,1:T(8,128)(2,1)} %fusion.15), calls=%async_computation.1 | async-start | bytes 393216 | tf_op jit(solution)/shard_map/all_to_all | solution.py:33
  256.7 1.6 gather_fusion.1
  258.3 1.5 copy.41
  259.9 6.7 %all-to-all-done.1 = bf16[8,32,320]{2,0,1:T(8,128)(2,1)S(1)} async-done(((bf16[8,32,320]{2,0,1:T(8,128)(2,1)}), bf16[8,32,320]{2,0,1:T(8,128)(2,1)S(1)}, u32[]{:S(2)}, u32[]{:S(2)}) %all-to-all-start.1) | async-done | bytes 163872 | tf_op jit(solution)/shard_map/all_to_all | solution.py:33
  266.6 0.2 reshape.211
  267.0 0.1 fusion.46
  267.3 0.3 fusion.31
  267.5 0.5 fusion.47
  268.1 0.3 fusion.22
  268.4 0.3 fusion.14
  268.8 0.7 copy.34
  269.5 4.3 %all-to-all-start.3 = ((bf16[8,32,256]{2,0,1:T(8,128)(2,1)}), bf16[8,32,256]{2,0,1:T(8,128)(2,1)S(1)}, u32[]{:S(2)}, u32[]{:S(2)}) async-start(bf16[8,32,256]{2,0,1:T(8,128)(2,1)} %copy.34), calls=%async_computation.3 | async-start | bytes 262144 | tf_op jit(solution)/shard_map/all_to_all | solution.py:33
  273.8 0.2 reduce-scatter.2.cloned.1.call-start
  274.0 8.9 %all-to-all-done.3 = bf16[8,32,256]{2,0,1:T(8,128)(2,1)S(1)} async-done(((bf16[8,32,256]{2,0,1:T(8,128)(2,1)}), bf16[8,32,256]{2,0,1:T(8,128)(2,1)S(1)}, u32[]{:S(2)}, u32[]{:S(2)}) %all-to-all-start.3) | async-done | bytes 131104 | tf_op jit(solution)/shard_map/all_to_all | solution.py:33
  282.9 3.4 fusion
  286.4 4.2 %copy.69 = bf16[32,8,8192]{2,1,0:T(8,128)(2,1)} copy(bf16[32,8,8192]{2,0,1:T(8,128)(2,1)S(1)} %fusion) | data formatting | bytes 8388608 | tf_op jit(solution)/shard_map/convert_element_type | solution.py:116
  290.6 118.4 %reduce-scatter.2.cloned.1.call-done = bf16[256,256]{1,0:T(8,128)(2,1)} async-done(((bf16[256,8192]{1,0:T(8,128)(2,1)}), bf16[256,256]{1,0:T(8,128)(2,1)}) %reduce-scatter.2.cloned.1.call-update) | async-done | bytes 131088 | tf_op jit(solution)/shard_map/reduce_scatter | solution.py:116
  (44 shorter events, 1.5 us)
Async XLA Ops:
  6.5 16.9 %copy-start = (bf16[32,2,8,1024]{3,2,1,0:T(8,128)(2,1)S(1)}, bf16[32,2,8,1024]{3,2,1,0:T(8,128)(2,1)}, u32[]{:S(2)}) copy-start(bf16[32,2,8,1024]{3,2,1,0:T(8,128)(2,1)} %param.12) | copy-start | bytes 3145732
  10.4 11.6 %copy-start.3 = (s32[1024,1]{0,1:T(1,128)S(1)}, s32[1024,1]{0,1:T(1,128)}, u32[]{:S(2)}) copy-start(s32[1024,1]{0,1:T(1,128)} %param.14) | copy-start | bytes 12292
  10.4 12.6 %copy-start.2 = (s32[1024]{0:T(1024)S(1)}, s32[1024]{0:T(1024)}, u32[]{:S(2)}) copy-start(s32[1024]{0:T(1024)} %param.15) | copy-start | bytes 12292
  10.4 177.0 %all-to-all-start = ((bf16[16,512,320]{1,2,0:T(8,128)(2,1)}), bf16[16,512,320]{1,2,0:T(8,128)(2,1)}, u32[]{:S(2)}, u32[]{:S(2)}) async-start(bf16[16,512,320]{1,2,0:T(8,128)(2,1)} %stack.2), calls=%async_computation | async-start | bytes 10485760 | tf_op jit(solution)/shard_map/all_to_all | solution.py:16
  20.8 253.2 %all-gather.2.cloned.1.call-start = ((), (), s32[]{:S(2)}) async-start(), calls=%async_computation.5 | async-start | bytes 4456448 | tf_op jit(solution)/shard_map/all_gather | solution.py:112
  23.4 174.2 %copy-start.1 = (bf16[8192]{0:T(1024)(128)(2,1)S(1)}, bf16[8192]{0:T(1024)(128)(2,1)}, u32[]{:S(2)}) copy-start(bf16[8192]{0:T(1024)(128)(2,1)} %param.9) | copy-start | bytes 49156
  23.5 174.3 %copy-start.4 = (s32[256]{0:T(256)S(1)}, s32[256]{0:T(256)}, u32[]{:S(2)}) copy-start(s32[256]{0:T(256)} %param.13) | copy-start | bytes 3076
  187.5 60.4 %all-to-all-start.2 = ((bf16[32,2,2,8,1024]{4,3,2,1,0:T(8,128)(2,1)}), bf16[32,2,2,8,1024]{4,3,2,1,0:T(8,128)(2,1)S(1)}, u32[]{:S(2)}, u32[]{:S(2)}) async-start(bf16[32,2,2,8,1024]{4,3,2,1,0:T(8,128)(2,1)} %bitcast.7), calls=%async_computation.2 | async-start | bytes 4194304 | tf_op jit(solution)/shard_map/all_to_all | solution.py:92
  247.9 18.6 %all-to-all-start.1 = ((bf16[8,32,320]{2,0,1:T(8,128)(2,1)}), bf16[8,32,320]{2,0,1:T(8,128)(2,1)S(1)}, u32[]{:S(2)}, u32[]{:S(2)}) async-start(bf16[8,32,320]{2,0,1:T(8,128)(2,1)} %fusion.15), calls=%async_computation.1 | async-start | bytes 393216 | tf_op jit(solution)/shard_map/all_to_all | solution.py:33
  269.5 13.4 %all-to-all-start.3 = ((bf16[8,32,256]{2,0,1:T(8,128)(2,1)}), bf16[8,32,256]{2,0,1:T(8,128)(2,1)S(1)}, u32[]{:S(2)}, u32[]{:S(2)}) async-start(bf16[8,32,256]{2,0,1:T(8,128)(2,1)} %copy.34), calls=%async_computation.3 | async-start | bytes 262144 | tf_op jit(solution)/shard_map/all_to_all | solution.py:33
  273.8 135.3 %reduce-scatter.2.cloned.1.call-start = ((), (), s32[]{:S(2)}) async-start(), calls=%async_computation.6 | async-start | bytes 4325376 | tf_op jit(solution)/shard_map/reduce_scatter | solution.py:116
Sparse Core Ops, SparseCore 0:
  24.6 162.0 all-gather.1
  290.8 118.2 reduce-scatter.1
